TPU v7x, 256 devices: a whole 4x4x8 slice. The times are simulated.
256 devices in a mesh: wide: 64 (over x, z, core), narrow: 4 (over y).
Axes of the slice: x: 4, y: 4, z: 8, core: 2. Of those that a mesh axis runs over, the one named last changes fastest.
Arguments:
- attn_heads: bfloat16 [8192, 1536], P('wide', 'narrow'), may hold values from -6 to 6
- w_out: bfloat16 [1536, 1536], P('narrow'), may hold values from -0.21875 to 0.21875
- residual: bfloat16 [8192, 1536], P('wide', 'narrow'), may hold values from -6 to 6
- norm_gain: float32 [1536], replicated, may hold values from 0.1 to 1.9
- route_ids: int32 [8192, 4], P('wide'), may hold values from 0 to 31, all different within a row; in each aligned block of 128 rows (0 to 127, 128 to 255, ...) at most 32 rows name the same one
- route_weight: float32 [8192, 4], P('wide'), may hold values from 0.1 to 1
- row_order: int32 [8192], P('wide'), may hold values from 0 to 8191, as said below
- slot_expert: int32 [64], replicated, may hold values from 0 to 31, as said below
- w_in: bfloat16 [64, 2, 768, 1536], P('wide', None, 'narrow')
- w_down: bfloat16 [64, 768, 1536], P('wide', 'narrow')
Outputs:
- block_out: bfloat16 [8192, 1536], P('wide', 'narrow')
Inputs may be any that keep to these rules, and one draw needn't show every extreme that they name: `route_ids`: each row names 4 different experts; among the 128 rows of one index of wide no expert is named more than 32 times. `row_order`: A permutation of the rows; of the 128 rows of each index of wide, exactly 2 have their initial position among the rows of each index of wide. `slot_expert`: every expert is held by one or more slots; slots holding the same expert hold equal w_in and w_down.
All inputs are finite; a program needn't handle non-finite values.
Results may differ from a plain program's by a relative error of at most 0.017.
Values may be sent and summed in bfloat16 or wider, within the bound.
No kernel may reach another device: no remote copies, remote signals or barrier semaphores. Data moves between devices by JAX's collectives and lax.ppermute only.
A program may use at most 128 MiB of HBM per device.

v0:
```python
import jax
import jax.numpy as jnp
from jax import lax
from jax.sharding import PartitionSpec as P

EXPERTS = 32
CAP = 32


def running_rank(onehot):
    return jnp.sum((jnp.cumsum(onehot, axis=0) - onehot) * onehot, axis=1)


def local(
    attn_heads,
    w_out,
    residual,
    norm_gain,
    route_ids,
    route_weight,
    row_order,
    slot_expert,
    w_in,
    w_down,
):
    row_count = residual.shape[0]
    wide_count = lax.axis_size("wide")
    narrow_count = lax.axis_size("narrow")
    width_local = residual.shape[1]
    model_width = width_local * narrow_count
    me_narrow = lax.axis_index("narrow")
    slot_local = w_in.shape[0]
    hid_local = w_down.shape[1]
    both = jnp.concatenate([w_in.reshape(slot_local, 2 * hid_local, model_width), w_down], axis=1)
    both = lax.all_gather(both, "narrow", axis=0, tiled=False)
    w_in_all = both[:, :, : 2 * hid_local].reshape(
        narrow_count, slot_local, 2, hid_local, model_width
    )
    w_down_all = both[:, :, 2 * hid_local :]
    partial_terms = jnp.dot(attn_heads, w_out, preferred_element_type=jnp.float32)
    projected = lax.psum_scatter(
        partial_terms.astype(jnp.bfloat16), "narrow", scatter_dimension=1, tiled=True
    ).astype(jnp.float32)
    hidden = (residual.astype(jnp.float32) + projected).astype(jnp.bfloat16)
    hidden_f = hidden.astype(jnp.float32)
    whole_rows = lax.all_gather(hidden, "narrow", axis=1, tiled=True).astype(jnp.float32)
    mean_sq = jnp.mean(whole_rows * whole_rows, axis=1, keepdims=True)
    normed = (whole_rows * lax.rsqrt(mean_sq + 1e-06) * norm_gain).astype(jnp.bfloat16)
    slot_count = slot_expert.shape[0]
    top_count = route_ids.shape[1]
    band = CAP // narrow_count
    held = (slot_expert[None, :] == jnp.arange(EXPERTS, dtype=jnp.int32)[:, None]).astype(jnp.int32)
    copies = jnp.sum(held, axis=1)
    replica_rank = jnp.cumsum(held, axis=1) - held
    flat_ids = route_ids.reshape(-1)
    choose_expert = (flat_ids[:, None] == jnp.arange(EXPERTS, dtype=jnp.int32)[None, :]).astype(
        jnp.int32
    )
    copy_count = jnp.sum(choose_expert * copies[None, :], axis=1)
    replica = jnp.repeat(row_order, top_count) % copy_count
    held_rows = jnp.sum(choose_expert[:, :, None] * held[None, :, :], axis=1)
    rank_rows = jnp.sum(choose_expert[:, :, None] * replica_rank[None, :, :], axis=1)
    slot_hit = held_rows * (rank_rows == replica[:, None]).astype(jnp.int32)
    slot_index = jnp.sum(slot_hit * jnp.arange(slot_count, dtype=jnp.int32)[None, :], axis=1)
    rank = running_rank(slot_hit)
    position = slot_index * CAP + rank
    send_at = jnp.where(
        rank // band == me_narrow, slot_index * band + rank % band, slot_count * band
    )
    outgoing = (
        jnp.zeros((slot_count * band, model_width), jnp.bfloat16)
        .at[send_at]
        .set(jnp.repeat(normed, top_count, axis=0), mode="drop")
    )
    outgoing = outgoing.reshape(wide_count, slot_local, band, model_width)
    arrived = lax.all_to_all(outgoing, "wide", split_axis=0, concat_axis=0, tiled=True)
    gate_up = jnp.einsum(
        "nscd,qsghd->nscgqh", arrived, w_in_all, preferred_element_type=jnp.float32
    )
    active = (jax.nn.relu(gate_up[:, :, :, 0]) * gate_up[:, :, :, 1]).astype(jnp.bfloat16)
    lowered = jnp.einsum(
        "nscqh,qshd->qnscd", active, w_down_all, preferred_element_type=jnp.float32
    )
    pieces = lowered.astype(jnp.bfloat16).astype(jnp.float32)
    summed = jnp.sum(pieces, axis=0).astype(jnp.bfloat16)
    summed = summed.reshape(wide_count, slot_local, band, narrow_count, width_local)
    summed = lax.all_to_all(summed, "narrow", split_axis=3, concat_axis=2, tiled=True)
    summed = summed.reshape(wide_count, slot_local, CAP, width_local)
    returned = lax.all_to_all(summed, "wide", split_axis=0, concat_axis=0, tiled=True)
    expert_out = returned.reshape(slot_count * CAP, width_local)[position]
    weighted = route_weight[:, :, None] * expert_out.reshape(
        row_count, top_count, width_local
    ).astype(jnp.float32)
    mixed = (hidden_f + jnp.sum(weighted, axis=1)).astype(jnp.bfloat16)
    pair_rows = row_count // wide_count
    target_dev = row_order // row_count
    target_place = row_order % row_count
    choose_target = (
        target_dev[:, None] == jnp.arange(wide_count, dtype=jnp.int32)[None, :]
    ).astype(jnp.int32)
    packed_index = target_dev * pair_rows + running_rank(choose_target)
    packed = jnp.zeros((row_count, width_local), jnp.bfloat16).at[packed_index].set(mixed)
    places = jnp.zeros((row_count,), jnp.int32).at[packed_index].set(target_place)
    assert row_count <= 256 and pair_rows <= width_local
    place_row = jnp.zeros((wide_count, 1, width_local), jnp.bfloat16)
    place_row = place_row.at[:, 0, :pair_rows].set(
        places.reshape(wide_count, pair_rows).astype(jnp.bfloat16)
    )
    packed = jnp.concatenate(
        [packed.reshape(wide_count, pair_rows, width_local), place_row], axis=1
    )
    arrived_all = lax.all_to_all(packed, "wide", split_axis=0, concat_axis=0, tiled=True)
    arrived_rows = arrived_all[:, :pair_rows]
    arrived_places = arrived_all[:, pair_rows, :pair_rows].astype(jnp.int32)
    return (
        jnp.zeros((row_count, width_local), jnp.bfloat16)
        .at[arrived_places.reshape(-1)]
        .set(arrived_rows.reshape(row_count, width_local))
    )


def solution(mesh):
    placed = (
        P("wide", "narrow"),
        P("narrow", None),
        P("wide", "narrow"),
        P(),
        P("wide", None),
        P("wide", None),
        P("wide"),
        P(),
        P("wide", None, "narrow", None),
        P("wide", "narrow", None),
    )
    return jax.shard_map(
        local, mesh=mesh, in_specs=placed, out_specs=P("wide", "narrow"), check_vma=False
    )
```

profile of v0, /device:TPU:1, one launch (start us, length us, event | category | flops | bytes accessed | tf_op | source)
XLA Modules:
  0.0 238.9 jit_solution(3613635565145867335)
XLA Ops:
  6.5 1.3 copy-done
  7.8 1.3 convolution_convert_fusion
  9.1 1.0 copy.54
  10.1 1.4 pad_maximum_fusion
  11.6 0.6 copy-done.6
  12.7 0.2 reduce_window_sum.38
  13.1 0.9 multiply_reduce_fusion.1
  14.2 1.2 reduce-window.6
  15.4 0.2 slice_reduce_fusion
  15.9 19.5 %reduce-scatter.4.cloned.1.call-done = bf16[384,128]{1,0:T(8,128)(2,1)} async-done(((bf16[1536,128]{1,0:T(8,128)(2,1)}), bf16[384,128]{1,0:T(8,128)(2,1)}) %reduce-scatter.4.cloned.1.call-update) | async-done | bytes 98320
  35.4 1.0 copy.55
  36.4 10.2 %all_gather.11 = bf16[128,1536]{1,0:T(8,128)(2,1)S(1)} all-gather(bf16[128,384]{1,0:T(8,128)(2,1)S(1)} %add_convert_fusion.1), channel_id=1, replica_groups=mesh['wide'=64,'narrow'=4] {'narrow'}, dimensions={1}, use_global_device_ids=true | all-gather | bytes 491520 | tf_op jit(solution)/shard_map/all_gather | solution.py:46
  47.0 0.4 broadcast_in_dim.24
  47.4 1.4 reshape.402
  48.8 5.2 %scatter_custom_fusion = bf16[512,1536]{1,0:T(8,128)(2,1)} fusion(s32[512]{0:T(512)S(1)} %bitcast.85, bf16[512,1536]{1,0:T(8,128)(2,1)} %reshape.402, bf16[]{:T(256)} %constant.111.clone.1), kind=kCustom, calls=%fused_computation.26 | custom fusion | bytes 1573376 | tf_op jit(solution)/shard_map/scatter | solution.py:73
  54.0 15.6 %all-to-all-start = ((bf16[64,1,8,1536]{3,2,1,0:T(8,128)(2,1)}), bf16[64,1,8,1536]{3,2,1,0:T(8,128)(2,1)S(1)}, u32[]{:S(2)}, u32[]{:S(2)}) async-start(bf16[64,1,8,1536]{3,2,1,0:T(8,128)(2,1)} %bitcast.14), calls=%async_computation | async-start | bytes 3145728 | tf_op jit(solution)/shard_map/all_to_all | solution.py:76
  69.6 44.3 %all-gather.3.cloned.1.call-done = bf16[4,576,1536]{2,1,0:T(8,128)(2,1)} async-done(((bf16[1,576,1536]{2,1,0:T(8,128)(2,1)}), bf16[4,576,1536]{2,1,0:T(8,128)(2,1)}) %all-gather.3.cloned.1.call-update) | async-done | bytes 7077904 | tf_op jit(solution)/shard_map/all_gather | solution.py:35
  114.0 4.9 %slice.58 = bf16[4,1,384,1536]{3,2,0,1:T(8,128)(2,1)} slice(bf16[4,1,576,1536]{3,2,0,1:T(8,128)(2,1)} %bitcast.75), slice={[0:4], [0:1], [0:384], [0:1536]} | slice | bytes 9437184 | tf_op jit(solution)/shard_map/slice | solution.py:36
  118.8 5.3 %convolution_bitcast_fusion = f32[64,1,8,2,4,192]{5,0,2,3,4,1:T(8,128)S(1)} fusion(bf16[4,2,192,1536,1]{3,2,4,1,0:T(8,128)(2,1)} %bitcast.74, bf16[64,1,8,1536]{3,2,1,0:T(8,128)(2,1)S(1)} %all-to-all-done), kind=kOutput, calls=%fused_computation.10 | convolution fusion | flops 2415919104 | bytes 9437184 | tf_op jit(solution)/shard_map/nscd,qsghd->nscgqh/dot_general | solution.py:77
  124.1 5.0 %convert_reduce_fusion = bf16[1536,64,8]{0,1,2:T(8,128)(2,1)} fusion(bf16[4,1,576,1536]{3,2,0,1:T(8,128)(2,1)} %bitcast.76, f32[64,1,8,2,4,192]{5,0,2,3,4,1:T(8,128)S(1)} %convolution_bitcast_fusion), kind=kOutput, calls=%fused_computation.5 | convolution fusion | flops 1214644224 | bytes 7077888 | tf_op jit(solution)/shard_map/nscqh,qshd->qnscd/dot_general | solution.py:81
  129.2 3.0 %reshape.436 = bf16[64,1,8,4,384]{4,3,0,2,1:T(4,128)(2,1)S(1)} reshape(bf16[64,8,1536]{2,0,1:T(8,128)(2,1)} %bitcast.77) | data formatting | bytes 3145728 | tf_op jit(solution)/shard_map/reshape | solution.py:86
  132.1 0.9 copy.45
  133.1 23.0 %all_to_all.30 = bf16[64,1,8,4,384]{4,2,0,1,3:T(8,128)(2,1)S(1)} all-to-all(bf16[64,1,8,4,384]{4,2,0,1,3:T(8,128)(2,1)S(1)} %copy.45), channel_id=1, replica_groups=mesh['wide'=64,'narrow'=4] {'narrow'}, dimensions={3} | all-to-all | bytes 3145728 | tf_op jit(solution)/shard_map/all_to_all | solution.py:87
  156.0 1.3 copy.66
  157.3 12.1 %all-to-all-start.2 = ((bf16[64,1,32,384]{3,2,1,0:T(8,128)(2,1)}), bf16[64,1,32,384]{3,2,1,0:T(8,128)(2,1)S(1)}, u32[]{:S(2)}, u32[]{:S(2)}) async-start(bf16[64,1,32,384]{3,2,1,0:T(8,128)(2,1)} %bitcast.73), calls=%async_computation.2 | async-start | bytes 3145728 | tf_op jit(solution)/shard_map/all_to_all | solution.py:89
  170.0 1.0 scatter_custom_fusion.2
  171.2 38.0 %all-to-all-done.2 = bf16[64,1,32,384]{3,2,1,0:T(8,128)(2,1)S(1)} async-done(((bf16[64,1,32,384]{3,2,1,0:T(8,128)(2,1)}), bf16[64,1,32,384]{3,2,1,0:T(8,128)(2,1)S(1)}, u32[]{:S(2)}, u32[]{:S(2)}) %all-to-all-start.2) | async-done | bytes 1572896 | tf_op jit(solution)/shard_map/all_to_all | solution.py:89
  209.2 1.9 gather_fusion
  211.3 0.5 multiply_reduce_fusion.2
  211.9 1.1 scatter_custom_fusion.1
  213.2 16.8 %all_to_all.31 = bf16[64,3,384]{2,1,0:T(4,128)(2,1)S(1)} all-to-all(bf16[64,3,384]{2,1,0:T(4,128)(2,1)S(1)} %fusion.12), channel_id=1, replica_groups=mesh['wide'=64,'narrow'=4] {'wide'}, dimensions={0} | all-to-all | bytes 294912 | tf_op jit(solution)/shard_map/all_to_all | solution.py:112
  230.4 1.6 scatter_custom_fusion.3
  (58 shorter events, 2.9 us)
Async XLA Ops:
  6.5 1.3 copy-start
  6.5 3.6 %copy-start.1 = (bf16[1,2,192,1536]{3,2,1,0:T(8,128)(2,1)S(1)}, bf16[1,2,192,1536]{3,2,1,0:T(8,128)(2,1)}, u32[]{:S(2)}) copy-start(bf16[1,2,192,1536]{3,2,1,0:T(8,128)(2,1)} %param.20) | copy-start | bytes 3538948
  6.5 3.6 %copy-start.2 = (bf16[1,192,1536]{2,1,0:T(8,128)(2,1)S(1)}, bf16[1,192,1536]{2,1,0:T(8,128)(2,1)}, u32[]{:S(2)}) copy-start(bf16[1,192,1536]{2,1,0:T(8,128)(2,1)} %param.21) | copy-start | bytes 1769476
  6.5 28.8 %reduce-scatter.4.cloned.1.call-start = ((), (), s32[]{:S(2)}) async-start(), calls=%async_computation.6 | async-start | bytes 491520
  10.1 103.9 %all-gather.3.cloned.1.call-start = ((), (), s32[]{:S(2)}) async-start(), calls=%async_computation.5 | async-start | bytes 8847360 | tf_op jit(solution)/shard_map/all_gather | solution.py:35
  11.6 0.7 copy-start.6
  11.6 0.9 copy-start.8
  11.6 1.1 copy-start.5
  11.6 24.8 %copy-start.3 = (bf16[128,384]{1,0:T(8,128)(2,1)S(1)}, bf16[128,384]{1,0:T(8,128)(2,1)}, u32[]{:S(2)}) copy-start(bf16[128,384]{1,0:T(8,128)(2,1)} %param.14) | copy-start | bytes 294916
  12.2 34.6 %copy-start.4 = (f32[1536]{0:T(1024)S(1)}, f32[1536]{0:T(1024)}, u32[]{:S(2)}) copy-start(f32[1536]{0:T(1024)} %param.15) | copy-start | bytes 18436
  54.0 64.9 %all-to-all-start = ((bf16[64,1,8,1536]{3,2,1,0:T(8,128)(2,1)}), bf16[64,1,8,1536]{3,2,1,0:T(8,128)(2,1)S(1)}, u32[]{:S(2)}, u32[]{:S(2)}) async-start(bf16[64,1,8,1536]{3,2,1,0:T(8,128)(2,1)} %bitcast.14), calls=%async_computation | async-start | bytes 3145728 | tf_op jit(solution)/shard_map/all_to_all | solution.py:76
  157.3 12.1 %copy-start.7 = (f32[128,4]{0,1:T(4,128)S(1)}, f32[128,4]{0,1:T(4,128)}, u32[]{:S(2)}) copy-start(f32[128,4]{0,1:T(4,128)} %param.17) | copy-start | bytes 6148
  157.3 51.8 %all-to-all-start.2 = ((bf16[64,1,32,384]{3,2,1,0:T(8,128)(2,1)}), bf16[64,1,32,384]{3,2,1,0:T(8,128)(2,1)S(1)}, u32[]{:S(2)}, u32[]{:S(2)}) async-start(bf16[64,1,32,384]{3,2,1,0:T(8,128)(2,1)} %bitcast.73), calls=%async_computation.2 | async-start | bytes 3145728 | tf_op jit(solution)/shard_map/all_to_all | solution.py:89
Sparse Core Ops, SparseCore 0:
  10.2 25.1 reduce-scatter.3
  37.2 76.7 all-gather.2
where the time goes:
time: 240 us; the launch traced here: 239 us
  waiting for transfers between devices  102 us (42%)
  blocking collectives  50 us (21%)
  starting transfers between devices  27.8 us (12%)
  local copies, waits for them, and re-layouts  26.9 us (11%)
  between operations  13.7 us (6%)
  matrix products  11.6 us (5%)
  other arithmetic  7.02 us (3%)
    all_gather x1, waiting for transfers between devices, local(): both = lax.all_gather(both, 'narrow', axis=0, tiled=False)  44.3 us
    all_to_all x1, waiting for transfers between devices, local(): lax.all_to_all(summed, 'wide', split_axis=0, concat_axis=0, tiled=True)  38 us
    all_to_all x1, blocking collectives, local(): lax.all_to_all(summed, 'narrow', split_axis=3, concat_axis=2, tiled=True)  23 us
    unnamed x3, waiting for transfers between devices  19.5 us
    all_to_all x1, blocking collectives, local(): lax.all_to_all(packed, 'wide', split_axis=0, concat_axis=0, tiled=True)  16.8 us
    all_to_all x1, starting transfers between devices, local(): lax.all_to_all(outgoing, 'wide', split_axis=0, concat_axis=0, tiled=True)  15.6 us
    all_to_all x1, starting transfers between devices, local(): lax.all_to_all(summed, 'wide', split_axis=0, concat_axis=0, tiled=True)  12.1 us
    all_gather x1, blocking collectives, local(): lax.all_gather(hidden, 'narrow', axis=1, tiled=True).astype(jnp.float32)  10.2 us
  transfers between devices with their start and end apart: 4, of which 3 were waited for; matrix products, arithmetic and copies ran while one was open for 8% of the time, Pallas kernels for 0%

commit v1 on v0

--- a/solution.py
+++ b/solution.py
@@ -43,7 +43,9 @@
     ).astype(jnp.float32)
     hidden = (residual.astype(jnp.float32) + projected).astype(jnp.bfloat16)
     hidden_f = hidden.astype(jnp.float32)
-    whole_rows = lax.all_gather(hidden, "narrow", axis=1, tiled=True).astype(jnp.float32)
+    whole_rows = jnp.concatenate(
+        lax.all_to_all(jnp.stack([hidden] * lax.axis_size("narrow")), "narrow", 0, 0), axis=1
+    ).astype(jnp.float32)
     mean_sq = jnp.mean(whole_rows * whole_rows, axis=1, keepdims=True)
     normed = (whole_rows * lax.rsqrt(mean_sq + 1e-06) * norm_gain).astype(jnp.bfloat16)
     slot_count = slot_expert.shape[0]

time: 240 us -> 240 us (level)
  blocking collectives: 50 us -> 39.8 us
  waiting for transfers between devices: 102 us -> 109 us
    all_gather x1 -> x0, blocking collectives: 10.2 us -> none  [local(): lax.all_gather(hidden, 'narrow', axis=1, tiled=True).astype(jnp.float32)]
    all_to_all x0 -> x1, waiting for transfers between devices: none -> 6.15 us  [local(): lax.all_to_all(jnp.stack([hidden] * lax.axis_size('narrow')), 'narrow', 0...]
    all_to_all x0 -> x1, starting transfers between devices: none -> 3.46 us  [local(): lax.all_to_all(jnp.stack([hidden] * lax.axis_size('narrow')), 'narrow', 0...]
  transfers between devices with their start and end apart: 4 -> 5, of which waited for: 3 -> 4; matrix products, arithmetic and copies ran while one was open for 8% -> 9% of each run, Pallas kernels for 0% -> 0%
where the time goes in v1:
time: 240 us; the launch traced here: 239 us
  waiting for transfers between devices  109 us (45%)
  blocking collectives  39.8 us (17%)
  starting transfers between devices  29.7 us (12%)
  local copies, waits for them, and re-layouts  28.3 us (12%)
  between operations  13.8 us (6%)
  matrix products  11.6 us (5%)
  other arithmetic  7.18 us (3%)
    all_gather x1, waiting for transfers between devices, local(): both = lax.all_gather(both, 'narrow', axis=0, tiled=False)  44.8 us
    all_to_all x1, waiting for transfers between devices, local(): lax.all_to_all(summed, 'wide', split_axis=0, concat_axis=0, tiled=True)  38 us
    all_to_all x1, blocking collectives, local(): lax.all_to_all(summed, 'narrow', split_axis=3, concat_axis=2, tiled=True)  23 us
    unnamed x3, waiting for transfers between devices  19.6 us
    all_to_all x1, blocking collectives, local(): lax.all_to_all(packed, 'wide', split_axis=0, concat_axis=0, tiled=True)  16.8 us
    all_to_all x1, starting transfers between devices, local(): lax.all_to_all(outgoing, 'wide', split_axis=0, concat_axis=0, tiled=True)  14.1 us
    all_to_all x1, starting transfers between devices, local(): lax.all_to_all(summed, 'wide', split_axis=0, concat_axis=0, tiled=True)  12.1 us
    all_to_all x1, waiting for transfers between devices, local(): lax.all_to_all(jnp.stack([hidden] * lax.axis_size('narrow')), 'narrow', 0...  6.15 us
  transfers between devices with their start and end apart: 5, of which 4 were waited for; matrix products, arithmetic and copies ran while one was open for 9% of the time, Pallas kernels for 0%

profile of v1, /device:TPU:1, one launch (start us, length us, event | category | flops | bytes accessed | tf_op | source)
XLA Modules:
  0.0 238.9 jit_solution(1588156797122013976)
XLA Ops:
  6.5 1.3 copy-done
  7.8 1.3 convolution_convert_fusion
  9.1 1.0 copy.69
  10.1 1.4 pad_maximum_fusion
  11.6 0.6 copy-done.6
  13.1 0.9 multiply_reduce_fusion.1
  14.2 1.2 reduce-window.6
  15.8 19.5 %reduce-scatter.4.cloned.1.call-done = bf16[384,128]{1,0:T(8,128)(2,1)} async-done(((bf16[1536,128]{1,0:T(8,128)(2,1)}), bf16[384,128]{1,0:T(8,128)(2,1)}) %reduce-scatter.4.cloned.1.call-update) | async-done | bytes 98320
  35.4 1.0 copy.70
  36.4 0.8 stack.2
  37.3 3.5 %all-to-all-start = ((bf16[4,128,384]{2,1,0:T(8,128)(2,1)}), bf16[4,128,384]{2,1,0:T(8,128)(2,1)S(1)}, u32[]{:S(2)}, u32[]{:S(2)}) async-start(bf16[4,128,384]{2,1,0:T(8,128)(2,1)} %stack.2), calls=%async_computation | async-start | bytes 786432 | tf_op jit(solution)/shard_map/all_to_all | solution.py:47
  40.8 6.1 %all-to-all-done = bf16[4,128,384]{2,1,0:T(8,128)(2,1)S(1)} async-done(((bf16[4,128,384]{2,1,0:T(8,128)(2,1)}), bf16[4,128,384]{2,1,0:T(8,128)(2,1)S(1)}, u32[]{:S(2)}, u32[]{:S(2)}) %all-to-all-start) | async-done | bytes 393248 | tf_op jit(solution)/shard_map/all_to_all | solution.py:47
  47.9 0.4 broadcast_in_dim.24
  48.3 1.4 reshape.409
  49.7 5.4 %scatter_custom_fusion = bf16[512,1536]{1,0:T(8,128)(2,1)} fusion(s32[512]{0:T(512)S(1)} %bitcast.93, bf16[512,1536]{1,0:T(8,128)(2,1)} %reshape.409, bf16[]{:T(256)} %constant.111.clone.1), kind=kCustom, calls=%fused_computation.25 | custom fusion | bytes 1573376 | tf_op jit(solution)/shard_map/scatter | solution.py:75
  55.0 14.1 %all-to-all-start.1 = ((bf16[64,1,8,1536]{3,2,1,0:T(8,128)(2,1)}), bf16[64,1,8,1536]{3,2,1,0:T(8,128)(2,1)S(1)}, u32[]{:S(2)}, u32[]{:S(2)}) async-start(bf16[64,1,8,1536]{3,2,1,0:T(8,128)(2,1)} %bitcast.16), calls=%async_computation.1 | async-start | bytes 3145728 | tf_op jit(solution)/shard_map/all_to_all | solution.py:78
  69.2 44.8 %all-gather.3.cloned.1.call-done = bf16[4,576,1536]{2,1,0:T(8,128)(2,1)} async-done(((bf16[1,576,1536]{2,1,0:T(8,128)(2,1)}), bf16[4,576,1536]{2,1,0:T(8,128)(2,1)}) %all-gather.3.cloned.1.call-update) | async-done | bytes 7077904 | tf_op jit(solution)/shard_map/all_gather | solution.py:35
  114.0 4.9 %slice.58 = bf16[4,1,384,1536]{3,2,0,1:T(8,128)(2,1)} slice(bf16[4,1,576,1536]{3,2,0,1:T(8,128)(2,1)} %bitcast.83), slice={[0:4], [0:1], [0:384], [0:1536]} | slice | bytes 9437184 | tf_op jit(solution)/shard_map/slice | solution.py:36
  118.8 5.3 %convolution_bitcast_fusion = f32[64,1,8,2,4,192]{5,0,2,3,4,1:T(8,128)S(1)} fusion(bf16[4,2,192,1536,1]{3,2,4,1,0:T(8,128)(2,1)} %bitcast.82, bf16[64,1,8,1536]{3,2,1,0:T(8,128)(2,1)S(1)} %all-to-all-done.1), kind=kOutput, calls=%fused_computation.10 | convolution fusion | flops 2415919104 | bytes 9437184 | tf_op jit(solution)/shard_map/nscd,qsghd->nscgqh/dot_general | solution.py:79
  124.2 5.0 %convert_reduce_fusion = bf16[1536,64,8]{0,1,2:T(8,128)(2,1)} fusion(bf16[4,1,576,1536]{3,2,0,1:T(8,128)(2,1)} %bitcast.84, f32[64,1,8,2,4,192]{5,0,2,3,4,1:T(8,128)S(1)} %convolution_bitcast_fusion), kind=kOutput, calls=%fused_computation.5 | convolution fusion | flops 1214644224 | bytes 7077888 | tf_op jit(solution)/shard_map/nscqh,qshd->qnscd/dot_general | solution.py:83
  129.2 3.0 %reshape.443 = bf16[64,1,8,4,384]{4,3,0,2,1:T(4,128)(2,1)S(1)} reshape(bf16[64,8,1536]{2,0,1:T(8,128)(2,1)} %bitcast.85) | data formatting | bytes 3145728 | tf_op jit(solution)/shard_map/reshape | solution.py:88
  132.2 0.9 copy.60
  133.1 23.0 %all_to_all.35 = bf16[64,1,8,4,384]{4,2,0,1,3:T(8,128)(2,1)S(1)} all-to-all(bf16[64,1,8,4,384]{4,2,0,1,3:T(8,128)(2,1)S(1)} %copy.60), channel_id=1, replica_groups=mesh['wide'=64,'narrow'=4] {'narrow'}, dimensions={3} | all-to-all | bytes 3145728 | tf_op jit(solution)/shard_map/all_to_all | solution.py:89
  156.1 1.3 copy.81
  157.4 12.1 %all-to-all-start.3 = ((bf16[64,1,32,384]{3,2,1,0:T(8,128)(2,1)}), bf16[64,1,32,384]{3,2,1,0:T(8,128)(2,1)S(1)}, u32[]{:S(2)}, u32[]{:S(2)}) async-start(bf16[64,1,32,384]{3,2,1,0:T(8,128)(2,1)} %bitcast.81), calls=%async_computation.3 | async-start | bytes 3145728 | tf_op jit(solution)/shard_map/all_to_all | solution.py:91
  170.1 1.0 scatter_custom_fusion.2
  171.2 38.0 %all-to-all-done.3 = bf16[64,1,32,384]{3,2,1,0:T(8,128)(2,1)S(1)} async-done(((bf16[64,1,32,384]{3,2,1,0:T(8,128)(2,1)}), bf16[64,1,32,384]{3,2,1,0:T(8,128)(2,1)S(1)}, u32[]{:S(2)}, u32[]{:S(2)}) %all-to-all-start.3) | async-done | bytes 1572896 | tf_op jit(solution)/shard_map/all_to_all | solution.py:91
  209.2 1.9 gather_fusion
  211.4 0.5 multiply_reduce_fusion.2
  211.9 1.1 scatter_custom_fusion.1
  213.2 16.8 %all_to_all.36 = bf16[64,3,384]{2,1,0:T(4,128)(2,1)S(1)} all-to-all(bf16[64,3,384]{2,1,0:T(4,128)(2,1)S(1)} %fusion.11), channel_id=1, replica_groups=mesh['wide'=64,'narrow'=4] {'wide'}, dimensions={0} | all-to-all | bytes 294912 | tf_op jit(solution)/shard_map/all_to_all | solution.py:114
  230.4 1.6 scatter_custom_fusion.3
  (62 shorter events, 4.0 us)
Async XLA Ops:
  6.5 1.3 copy-start
  6.5 3.6 %copy-start.1 = (bf16[1,2,192,1536]{3,2,1,0:T(8,128)(2,1)S(1)}, bf16[1,2,192,1536]{3,2,1,0:T(8,128)(2,1)}, u32[]{:S(2)}) copy-start(bf16[1,2,192,1536]{3,2,1,0:T(8,128)(2,1)} %param.20) | copy-start | bytes 3538948
  6.5 3.6 %copy-start.2 = (bf16[1,192,1536]{2,1,0:T(8,128)(2,1)S(1)}, bf16[1,192,1536]{2,1,0:T(8,128)(2,1)}, u32[]{:S(2)}) copy-start(bf16[1,192,1536]{2,1,0:T(8,128)(2,1)} %param.21) | copy-start | bytes 1769476
  6.5 28.8 %reduce-scatter.4.cloned.1.call-start = ((), (), s32[]{:S(2)}) async-start(), calls=%async_computation.7 | async-start | bytes 491520
  10.1 103.9 %all-gather.3.cloned.1.call-start = ((), (), s32[]{:S(2)}) async-start(), calls=%async_computation.6 | async-start | bytes 8847360 | tf_op jit(solution)/shard_map/all_gather | solution.py:35
  11.6 0.7 copy-start.6
  11.6 0.9 copy-start.8
  11.6 1.1 copy-start.5
  11.6 24.8 %copy-start.3 = (bf16[128,384]{1,0:T(8,128)(2,1)S(1)}, bf16[128,384]{1,0:T(8,128)(2,1)}, u32[]{:S(2)}) copy-start(bf16[128,384]{1,0:T(8,128)(2,1)} %param.14) | copy-start | bytes 294916
  14.2 33.2 %copy-start.4 = (f32[1536]{0:T(1024)S(1)}, f32[1536]{0:T(1024)}, u32[]{:S(2)}) copy-start(f32[1536]{0:T(1024)} %param.15) | copy-start | bytes 18436
  37.3 9.7 %all-to-all-start = ((bf16[4,128,384]{2,1,0:T(8,128)(2,1)}), bf16[4,128,384]{2,1,0:T(8,128)(2,1)S(1)}, u32[]{:S(2)}, u32[]{:S(2)}) async-start(bf16[4,128,384]{2,1,0:T(8,128)(2,1)} %stack.2), calls=%async_computation | async-start | bytes 786432 | tf_op jit(solution)/shard_map/all_to_all | solution.py:47
  55.0 63.8 %all-to-all-start.1 = ((bf16[64,1,8,1536]{3,2,1,0:T(8,128)(2,1)}), bf16[64,1,8,1536]{3,2,1,0:T(8,128)(2,1)S(1)}, u32[]{:S(2)}, u32[]{:S(2)}) async-start(bf16[64,1,8,1536]{3,2,1,0:T(8,128)(2,1)} %bitcast.16), calls=%async_computation.1 | async-start | bytes 3145728 | tf_op jit(solution)/shard_map/all_to_all | solution.py:78
  157.4 12.1 %copy-start.7 = (f32[128,4]{0,1:T(4,128)S(1)}, f32[128,4]{0,1:T(4,128)}, u32[]{:S(2)}) copy-start(f32[128,4]{0,1:T(4,128)} %param.17) | copy-start | bytes 6148
  157.4 51.9 %all-to-all-start.3 = ((bf16[64,1,32,384]{3,2,1,0:T(8,128)(2,1)}), bf16[64,1,32,384]{3,2,1,0:T(8,128)(2,1)S(1)}, u32[]{:S(2)}, u32[]{:S(2)}) async-start(bf16[64,1,32,384]{3,2,1,0:T(8,128)(2,1)} %bitcast.81), calls=%async_computation.3 | async-start | bytes 3145728 | tf_op jit(solution)/shard_map/all_to_all | solution.py:91
Sparse Core Ops, SparseCore 0:
  10.2 25.1 reduce-scatter.3
  37.2 76.7 all-gather.2
